TPU v7x, 256 devices: a whole 4x4x8 slice. The times are simulated.
256 devices in a mesh: dp: 16 (over y_hi, z), seq: 16 (over x, y_lo, core).
Axes of the slice: x: 4, y: 4 (y_hi: 2, y_lo: 2; y = y_hi * 2 + y_lo), z: 8, core: 2. Of those that a mesh axis runs over, the one named last changes fastest.
Arguments:
- queries: bfloat16 [16, 2048, 2048], P('dp', 'seq'), may hold values from -6 to 6
- key_states: bfloat16 [16, 2048, 2048], P('dp', 'seq'), may hold values from -6 to 6
- value_states: bfloat16 [16, 2048, 2048], P('dp', 'seq'), may hold values from -6 to 6
- cotangent: bfloat16 [16, 2048, 2048], P('dp', 'seq'), may hold values from -6 to 6
- filter_taps: float32 [7, 2048], replicated, may hold values from -3 to 3
Outputs:
- conv_output: bfloat16 [16, 2048, 2048], P('dp', 'seq')
- grad_queries: bfloat16 [16, 2048, 2048], P('dp', 'seq')
- grad_keys: bfloat16 [16, 2048, 2048], P('dp', 'seq')
- grad_values: bfloat16 [16, 2048, 2048], P('dp', 'seq')
- filter_gradient: float32 [7, 2048], replicated
All inputs are finite; a program needn't handle non-finite values.
Results may differ from a plain program's by a relative error of at most 0.015.
Values may be sent and summed in bfloat16 or wider, within the bound.
No kernel may reach another device: no remote copies, remote signals or barrier semaphores. Data moves between devices by JAX's collectives and lax.ppermute only.
A program may use at most 128 MiB of HBM per device.

v0:
```python
import math
import jax
import jax.numpy as jnp
from jax import lax
from jax.sharding import PartitionSpec as P

HD = 128
TAPS = 7


def padded(value, sides, width):
    for axis, dim in sides:
        peers, length = (lax.axis_size(axis), value.shape[dim])
        up = [(i, (i + 1) % peers) for i in range(peers)]
        down = [(j, i) for i, j in up]
        last = lax.slice_in_dim(value, length - width, length, axis=dim)
        leading = lax.slice_in_dim(value, 0, width, axis=dim)
        before = lax.ppermute(last, axis, up)
        after = lax.ppermute(leading, axis, down)
        value = jnp.concatenate([before, value, after], axis=dim)
    return value


def on_device(queries, key_states, value_states, cotangent, filter_taps):
    tok_rows = queries.shape[1]
    channels = queries.shape[2]
    sequence_shards = lax.axis_size("seq")
    seq_total = tok_rows * sequence_shards
    head_count = channels // HD
    group_heads = math.gcd(head_count, 4)
    group_width = group_heads * HD
    group_count = head_count // group_heads
    score_scale = HD ** (-0.5)
    half_width = (TAPS - 1) // 2
    local_q = queries[0]
    local_k = key_states[0]
    local_v = value_states[0]
    local_g = cotangent[0]
    grad_pad = padded(local_g, (("seq", 0),), half_width)
    grad_sum = jnp.zeros((tok_rows, channels), jnp.float32)
    for tap_index in range(TAPS):
        start_row = 2 * half_width - tap_index
        grad_sum = grad_sum + filter_taps[tap_index] * grad_pad[
            start_row : start_row + tok_rows
        ].astype(jnp.float32)
    grad_attn = grad_sum.astype(jnp.bfloat16)
    key_all, value_all = (
        lax.all_gather(local_k, "seq", axis=0, tiled=True),
        lax.all_gather(local_v, "seq", axis=0, tiled=True),
    )
    device_index = lax.axis_index("seq")
    query_pos = device_index * tok_rows + jnp.arange(tok_rows, dtype=jnp.int32)
    key_pos = jnp.arange(seq_total, dtype=jnp.int32)
    visible = query_pos[:, None] >= key_pos[None, :]

    def columns(matrix, group_index, count):
        picked = lax.dynamic_slice_in_dim(matrix, group_index * group_width, group_width, 1)
        return picked.reshape(count, group_heads, HD)

    def forward_group(group_index):
        q_part = columns(local_q, group_index, tok_rows)
        k_part = columns(key_all, group_index, seq_total)
        v_part = columns(value_all, group_index, seq_total)
        delta_portion = columns(grad_attn, group_index, tok_rows)
        scores = (
            jnp.einsum("thd,uhd->htu", q_part, k_part, preferred_element_type=jnp.float32)
            * score_scale
        )
        row_top = jnp.max(jnp.where(visible, scores, -jnp.inf), -1, keepdims=True)
        raw = jnp.where(visible, jnp.exp(scores - row_top), 0.0)
        row_total = jnp.sum(raw, -1, keepdims=True)
        probs = raw / row_total
        probs_low = probs.astype(jnp.bfloat16)
        attended = jnp.einsum("htu,uhd->thd", probs_low, v_part, preferred_element_type=jnp.float32)
        attended = attended.astype(jnp.bfloat16).reshape(tok_rows, group_width)
        dprob = jnp.einsum(
            "thd,uhd->htu", delta_portion, v_part, preferred_element_type=jnp.float32
        )
        row_delta = jnp.sum(probs * dprob, -1, keepdims=True)
        dscore = (probs * (dprob - row_delta) * score_scale).astype(jnp.bfloat16)
        grad_q = jnp.einsum("htu,uhd->thd", dscore, k_part, preferred_element_type=jnp.float32)
        grad_q = grad_q.astype(jnp.bfloat16).reshape(tok_rows, group_width)
        key_term = jnp.einsum("htu,thd->uhd", dscore, q_part, preferred_element_type=jnp.float32)
        value_term = jnp.einsum(
            "htu,thd->uhd", probs_low, delta_portion, preferred_element_type=jnp.float32
        )
        return (
            attended,
            grad_q,
            key_term.reshape(seq_total, group_width),
            value_term.reshape(seq_total, group_width),
        )

    group_ids = jnp.arange(group_count, dtype=jnp.int32)
    attended, grad_q, key_term, value_term = lax.map(forward_group, group_ids)
    key_share, value_share = (
        lax.psum_scatter(
            key_term.astype(jnp.bfloat16), "seq", scatter_dimension=1, tiled=True
        ).astype(jnp.float32),
        lax.psum_scatter(
            value_term.astype(jnp.bfloat16), "seq", scatter_dimension=1, tiled=True
        ).astype(jnp.float32),
    )
    grad_keys = key_share.transpose(1, 0, 2).reshape(tok_rows, channels).astype(jnp.bfloat16)
    grad_values = value_share.transpose(1, 0, 2).reshape(tok_rows, channels).astype(jnp.bfloat16)
    attn_out = attended.transpose(1, 0, 2).reshape(tok_rows, channels)
    grad_queries = grad_q.transpose(1, 0, 2).reshape(tok_rows, channels)
    out_pad = padded(attn_out, (("seq", 0),), half_width)
    conv_sum = jnp.zeros((tok_rows, channels), jnp.float32)
    filter_rows = []
    local_gf = local_g.astype(jnp.float32)
    for tap_index in range(TAPS):
        moved = out_pad[tap_index : tap_index + tok_rows].astype(jnp.float32)
        conv_sum = conv_sum + filter_taps[tap_index] * moved
        filter_rows.append(jnp.sum(moved * local_gf, 0))
    filter_gradient = lax.psum(jnp.stack(filter_rows, 0), ("dp", "seq"))
    conv_output = conv_sum.astype(jnp.bfloat16)
    return (
        conv_output[None],
        grad_queries[None],
        grad_keys[None],
        grad_values[None],
        filter_gradient,
    )


def solution(mesh):
    in_specs = (
        P("dp", "seq", None),
        P("dp", "seq", None),
        P("dp", "seq", None),
        P("dp", "seq", None),
        P(),
    )
    out_specs = (
        P("dp", "seq", None),
        P("dp", "seq", None),
        P("dp", "seq", None),
        P("dp", "seq", None),
        P(),
    )
    return jax.shard_map(
        on_device, mesh=mesh, in_specs=in_specs, out_specs=out_specs, check_vma=False
    )
```

profile of v0, /device:TPU:1, one launch (start us, length us, event | category | flops | bytes accessed | tf_op | source)
XLA Modules:
  0.0 557.8 jit_solution(18201332075401801703)
XLA Ops:
  7.2 2.1 copy.41
  9.4 2.0 copy.43
  12.3 2.8 collective-permute-start.1
  17.1 2.0 copy.42
  19.1 1.7 fusion.47
  20.9 57.9 %all-gather.5.cloned.1.call-done = bf16[1,2048,2048]{1,2,0:T(8,128)(2,1)} async-done(((bf16[1,128,2048]{1,2,0:T(8,128)(2,1)}), bf16[1,2048,2048]{1,2,0:T(8,128)(2,1)}) %all-gather.5.cloned.1.call-update) | async-done | bytes 8388624 | tf_op jit(solution)/shard_map/all_gather | solution.py:49
  78.7 65.4 %all-gather.7.cloned.1.call-done = bf16[1,2048,2048]{1,2,0:T(8,128)(2,1)} async-done(((bf16[1,128,2048]{1,2,0:T(8,128)(2,1)}), bf16[1,2048,2048]{1,2,0:T(8,128)(2,1)}) %all-gather.7.cloned.1.call-update) | async-done | bytes 8388624 | tf_op jit(solution)/shard_map/all_gather | solution.py:48
  144.2 177.4 %while.17 = (s32[]{:T(128)}, bf16[4,128,512]{1,2,0:T(8,128)(2,1)S(1)}, bf16[4,128,512]{1,2,0:T(8,128)(2,1)}, bf16[4,2048,512]{1,2,0:T(8,128)(2,1)}, bf16[4,2048,...) while((s32[]{:T(128)}, ...), condition=%wide.region_4.5_spmd.clone, body=%wide.region_0.4_spmd.clone.sunk | while | flops 1904614400 | bytes 82324224 | solution.py:95
  145.5 3.2 constant_dynamic-slice_fusion.8
  149.7 1.7 constant_dynamic-slice_fusion.10
  151.5 2.8 fusion.110
  155.4 6.5 %fusion.111 = (f32[4,128]{1,0:T(4,128)S(1)}, f32[4,128,2048]{2,1,0:T(8,128)}) fusion(pred[128,2048]{1,0:T(8,128)(4,1)S(1)} %iota_compare_fusion.2, bf16[128,4,128]{0,2,1:T(8,128)(2,1)S(1)} %bitcast.143, bf16[2048,4,128]{0,2,1:T(8,128)(2,1)} %bitcast.125), kind=kOutput, calls=%fused_computation.95.clone.1 | convolution fusion | flops 543164416 | bytes 6686720 | tf_op jit(solution)/shard_map/while/body/eval_jaxpr/sub | solution.py:70
  161.9 8.5 %fusion.112 = bf16[4,128,128]{2,1,0:T(8,128)(2,1)S(1)} fusion(bf16[2048,4,128]{0,2,1:T(8,128)(2,1)} %bitcast.126, f32[4,128,2048]{2,1,0:T(8,128)} %fusion.110, f32[4,128,2048]{2,1,0:T(8,128)} %get-tuple-element.242, f32[4,128]{1,0:T(4,128)S(1)} %get-tuple-element.243), kind=kOutput, calls=%fused_computation.18.clone.1 | convolution fusion | flops 275843584 | bytes 10618880 | tf_op jit(solution)/shard_map/while/body/eval_jaxpr/htu,uhd->thd/dot_general | solution.py:81
  170.5 3.1 convolution_convert_fusion.2
  175.1 9.5 %fusion.114 = bf16[4,128,2048]{2,1,0:T(8,128)(2,1)} fusion(bf16[128,4,128]{0,2,1:T(8,128)(2,1)S(1)} %bitcast.144, f32[4,128,2048]{2,1,0:T(8,128)} %fusion.110, f32[4,128,2048]{2,1,0:T(8,128)} %get-tuple-element.242, f32[4,128]{1,0:T(4,128)S(1)} %get-tuple-element.243), kind=kOutput, calls=%fused_computation.10.clone.1 | convolution fusion | flops 275778048 | bytes 10618880 | tf_op jit(solution)/shard_map/while/body/eval_jaxpr/htu,thd->uhd/dot_general | solution.py:83
  184.6 4.0 constant_dynamic-update-slice_fusion.7
  189.8 3.2 constant_dynamic-slice_fusion.8
  194.1 1.7 constant_dynamic-slice_fusion.10
  195.8 2.8 fusion.110
  199.7 6.5 %fusion.111 = (f32[4,128]{1,0:T(4,128)S(1)}, f32[4,128,2048]{2,1,0:T(8,128)}) fusion(pred[128,2048]{1,0:T(8,128)(4,1)S(1)} %iota_compare_fusion.2, bf16[128,4,128]{0,2,1:T(8,128)(2,1)S(1)} %bitcast.143, bf16[2048,4,128]{0,2,1:T(8,128)(2,1)} %bitcast.125), kind=kOutput, calls=%fused_computation.95.clone.1 | convolution fusion | flops 543164416 | bytes 6686720 | tf_op jit(solution)/shard_map/while/body/eval_jaxpr/sub | solution.py:70
  206.3 8.5 %fusion.112 = bf16[4,128,128]{2,1,0:T(8,128)(2,1)S(1)} fusion(bf16[2048,4,128]{0,2,1:T(8,128)(2,1)} %bitcast.126, f32[4,128,2048]{2,1,0:T(8,128)} %fusion.110, f32[4,128,2048]{2,1,0:T(8,128)} %get-tuple-element.242, f32[4,128]{1,0:T(4,128)S(1)} %get-tuple-element.243), kind=kOutput, calls=%fused_computation.18.clone.1 | convolution fusion | flops 275843584 | bytes 10618880 | tf_op jit(solution)/shard_map/while/body/eval_jaxpr/htu,uhd->thd/dot_general | solution.py:81
  214.8 3.1 convolution_convert_fusion.2
  219.4 9.5 %fusion.114 = bf16[4,128,2048]{2,1,0:T(8,128)(2,1)} fusion(bf16[128,4,128]{0,2,1:T(8,128)(2,1)S(1)} %bitcast.144, f32[4,128,2048]{2,1,0:T(8,128)} %fusion.110, f32[4,128,2048]{2,1,0:T(8,128)} %get-tuple-element.242, f32[4,128]{1,0:T(4,128)S(1)} %get-tuple-element.243), kind=kOutput, calls=%fused_computation.10.clone.1 | convolution fusion | flops 275778048 | bytes 10618880 | tf_op jit(solution)/shard_map/while/body/eval_jaxpr/htu,thd->uhd/dot_general | solution.py:83
  228.9 4.0 constant_dynamic-update-slice_fusion.7
  234.2 3.2 constant_dynamic-slice_fusion.8
  238.4 1.7 constant_dynamic-slice_fusion.10
  240.1 2.8 fusion.110
  244.1 6.5 %fusion.111 = (f32[4,128]{1,0:T(4,128)S(1)}, f32[4,128,2048]{2,1,0:T(8,128)}) fusion(pred[128,2048]{1,0:T(8,128)(4,1)S(1)} %iota_compare_fusion.2, bf16[128,4,128]{0,2,1:T(8,128)(2,1)S(1)} %bitcast.143, bf16[2048,4,128]{0,2,1:T(8,128)(2,1)} %bitcast.125), kind=kOutput, calls=%fused_computation.95.clone.1 | convolution fusion | flops 543164416 | bytes 6686720 | tf_op jit(solution)/shard_map/while/body/eval_jaxpr/sub | solution.py:70
  250.6 8.5 %fusion.112 = bf16[4,128,128]{2,1,0:T(8,128)(2,1)S(1)} fusion(bf16[2048,4,128]{0,2,1:T(8,128)(2,1)} %bitcast.126, f32[4,128,2048]{2,1,0:T(8,128)} %fusion.110, f32[4,128,2048]{2,1,0:T(8,128)} %get-tuple-element.242, f32[4,128]{1,0:T(4,128)S(1)} %get-tuple-element.243), kind=kOutput, calls=%fused_computation.18.clone.1 | convolution fusion | flops 275843584 | bytes 10618880 | tf_op jit(solution)/shard_map/while/body/eval_jaxpr/htu,uhd->thd/dot_general | solution.py:81
  259.2 3.1 convolution_convert_fusion.2
  263.8 9.5 %fusion.114 = bf16[4,128,2048]{2,1,0:T(8,128)(2,1)} fusion(bf16[128,4,128]{0,2,1:T(8,128)(2,1)S(1)} %bitcast.144, f32[4,128,2048]{2,1,0:T(8,128)} %fusion.110, f32[4,128,2048]{2,1,0:T(8,128)} %get-tuple-element.242, f32[4,128]{1,0:T(4,128)S(1)} %get-tuple-element.243), kind=kOutput, calls=%fused_computation.10.clone.1 | convolution fusion | flops 275778048 | bytes 10618880 | tf_op jit(solution)/shard_map/while/body/eval_jaxpr/htu,thd->uhd/dot_general | solution.py:83
  273.3 4.0 constant_dynamic-update-slice_fusion.7
  278.5 3.2 constant_dynamic-slice_fusion.8
  282.7 1.7 constant_dynamic-slice_fusion.10
  284.5 2.8 fusion.110
  288.4 6.5 %fusion.111 = (f32[4,128]{1,0:T(4,128)S(1)}, f32[4,128,2048]{2,1,0:T(8,128)}) fusion(pred[128,2048]{1,0:T(8,128)(4,1)S(1)} %iota_compare_fusion.2, bf16[128,4,128]{0,2,1:T(8,128)(2,1)S(1)} %bitcast.143, bf16[2048,4,128]{0,2,1:T(8,128)(2,1)} %bitcast.125), kind=kOutput, calls=%fused_computation.95.clone.1 | convolution fusion | flops 543164416 | bytes 6686720 | tf_op jit(solution)/shard_map/while/body/eval_jaxpr/sub | solution.py:70
  294.9 8.5 %fusion.112 = bf16[4,128,128]{2,1,0:T(8,128)(2,1)S(1)} fusion(bf16[2048,4,128]{0,2,1:T(8,128)(2,1)} %bitcast.126, f32[4,128,2048]{2,1,0:T(8,128)} %fusion.110, f32[4,128,2048]{2,1,0:T(8,128)} %get-tuple-element.242, f32[4,128]{1,0:T(4,128)S(1)} %get-tuple-element.243), kind=kOutput, calls=%fused_computation.18.clone.1 | convolution fusion | flops 275843584 | bytes 10618880 | tf_op jit(solution)/shard_map/while/body/eval_jaxpr/htu,uhd->thd/dot_general | solution.py:81
  303.5 3.1 convolution_convert_fusion.2
  308.1 9.5 %fusion.114 = bf16[4,128,2048]{2,1,0:T(8,128)(2,1)} fusion(bf16[128,4,128]{0,2,1:T(8,128)(2,1)S(1)} %bitcast.144, f32[4,128,2048]{2,1,0:T(8,128)} %fusion.110, f32[4,128,2048]{2,1,0:T(8,128)} %get-tuple-element.242, f32[4,128]{1,0:T(4,128)S(1)} %get-tuple-element.243), kind=kOutput, calls=%fused_computation.10.clone.1 | convolution fusion | flops 275778048 | bytes 10618880 | tf_op jit(solution)/shard_map/while/body/eval_jaxpr/htu,thd->uhd/dot_general | solution.py:83
  317.6 4.0 constant_dynamic-update-slice_fusion.7
  321.6 14.6 %copy.60 = bf16[4,2048,512]{2,0,1:T(4,128)(2,1)} copy(bf16[4,2048,512]{1,2,0:T(8,128)(2,1)} %get-tuple-element.67) | data formatting | bytes 16777216
  336.2 10.2 %copy.65 = bf16[256,8,4,512]{3,1,2,0:T(8,128)(2,1)} copy(bf16[256,8,4,512]{3,2,1,0:T(4,128)(2,1)} %bitcast.131) | data formatting | bytes 16777216
  346.5 14.6 %copy.62 = bf16[4,2048,512]{2,0,1:T(4,128)(2,1)} copy(bf16[4,2048,512]{1,2,0:T(8,128)(2,1)} %get-tuple-element.68) | data formatting | bytes 16777216
  361.0 10.2 %copy.66 = bf16[256,8,4,512]{3,1,2,0:T(8,128)(2,1)} copy(bf16[256,8,4,512]{3,2,1,0:T(4,128)(2,1)} %bitcast.132) | data formatting | bytes 16777216
  375.9 2.0 copy.59
  379.1 78.2 %psum.7 = f32[7,2048]{1,0:T(8,128)} all-reduce(f32[7,2048]{1,0:T(8,128)S(1)} %stack.31), channel_id=1, replica_groups=mesh['dp'=16,'seq'=16] {'dp','seq'}, use_global_device_ids=true, to_apply=%region_14.15 | all-reduce | flops 14336 | bytes 114688 | tf_op jit(solution)/shard_map/psum | solution.py:116
  457.4 1.7 fusion.62
  462.0 86.5 %reduce-scatter.9.cloned.1.call-done = bf16[128,2048]{1,0:T(8,128)(2,1)} async-done(((bf16[2048,2048]{1,0:T(8,128)(2,1)}), bf16[128,2048]{1,0:T(8,128)(2,1)}) %reduce-scatter.9.cloned.1.call-update) | async-done | bytes 524304
  (107 shorter events, 31.1 us)
Async XLA Ops:
  7.2 11.9 %copy-start = (bf16[1,128,2048]{2,1,0:T(8,128)(2,1)S(1)}, bf16[1,128,2048]{2,1,0:T(8,128)(2,1)}, u32[]{:S(2)}) copy-start(bf16[1,128,2048]{2,1,0:T(8,128)(2,1)} %param.10) | copy-start | bytes 1572868
  7.2 71.6 %all-gather.5.cloned.1.call-start = ((), (), s32[]{:S(2)}) async-start(), calls=%async_computation.2 | async-start | bytes 8912896 | tf_op jit(solution)/shard_map/all_gather | solution.py:49
  9.3 134.8 %all-gather.7.cloned.1.call-start = ((), (), s32[]{:S(2)}) async-start(), calls=%async_computation.3 | async-start | bytes 8912896 | tf_op jit(solution)/shard_map/all_gather | solution.py:48
  11.5 447.6 %reduce-scatter.7.cloned.1.call-start = ((), (), s32[]{:S(2)}) async-start(), calls=%async_computation.4 | async-start | bytes 8912896
  12.3 6.8 %collective-permute-start.1 = (bf16[3,2048]{1,0:T(4,128)(2,1)S(1)}, bf16[3,2048]{1,0:T(4,128)(2,1)S(1)}, u32[]{:S(2)}, u32[]{:S(2)}) collective-permute-start(bf16[3,2048]{1,0:T(4,128)(2,1)S(1)} %get-tuple-element.161), channel_id=1, source_target_pairs={{0,1},{1,2},{2,3},{3,4},{4,5},{5,6},{6,7},{7,8},{8,9},{9,10},{10,1... | collective-permute-start | bytes 36872 | tf_op jit(solution)/shard_map/ppermute | solution.py:18
  15.1 4.0 collective-permute-start
  16.9 127.2 %copy-start.2 = (f32[1,2048]{1,0:T(1,128)}, f32[1,2048]{1,0:T(1,128)S(1)}, u32[]{:S(2)}) copy-start(f32[1,2048]{1,0:T(1,128)S(1)} %get-tuple-element.162) | copy-start | bytes 24580
  16.9 127.2 %copy-start.4 = (f32[1,2048]{1,0:T(1,128)}, f32[1,2048]{1,0:T(1,128)S(1)}, u32[]{:S(2)}) copy-start(f32[1,2048]{1,0:T(1,128)S(1)} %get-tuple-element.163) | copy-start | bytes 24580
  16.9 127.2 %copy-start.6 = (f32[1,2048]{1,0:T(1,128)}, f32[1,2048]{1,0:T(1,128)S(1)}, u32[]{:S(2)}) copy-start(f32[1,2048]{1,0:T(1,128)S(1)} %get-tuple-element.164) | copy-start | bytes 24580
  17.0 127.2 %copy-start.8 = (f32[1,2048]{1,0:T(1,128)}, f32[1,2048]{1,0:T(1,128)S(1)}, u32[]{:S(2)}) copy-start(f32[1,2048]{1,0:T(1,128)S(1)} %get-tuple-element.165) | copy-start | bytes 24580
  17.0 127.2 %copy-start.10 = (f32[1,2048]{1,0:T(1,128)}, f32[1,2048]{1,0:T(1,128)S(1)}, u32[]{:S(2)}) copy-start(f32[1,2048]{1,0:T(1,128)S(1)} %get-tuple-element.166) | copy-start | bytes 24580
  17.0 127.2 %copy-start.12 = (f32[1,2048]{1,0:T(1,128)}, f32[1,2048]{1,0:T(1,128)S(1)}, u32[]{:S(2)}) copy-start(f32[1,2048]{1,0:T(1,128)S(1)} %get-tuple-element.167) | copy-start | bytes 24580
  17.0 127.2 %copy-start.14 = (f32[1,2048]{1,0:T(1,128)}, f32[1,2048]{1,0:T(1,128)S(1)}, u32[]{:S(2)}) copy-start(f32[1,2048]{1,0:T(1,128)S(1)} %get-tuple-element.168) | copy-start | bytes 24580
  170.5 3.8 copy-start.16
  214.8 3.8 copy-start.16
  259.1 3.8 copy-start.16
  303.5 3.8 copy-start.16
  346.4 202.0 %reduce-scatter.9.cloned.1.call-start = ((), (), s32[]{:S(2)}) async-start(), calls=%async_computation.5 | async-start | bytes 8912896
  371.3 1.0 copy-start.1
  372.5 84.8 %copy-start.3 = (f32[1,2048]{1,0:T(1,128)S(1)}, f32[1,2048]{1,0:T(1,128)}, u32[]{:S(2)}) copy-start(f32[1,2048]{1,0:T(1,128)} %copy-done.2) | copy-start | bytes 24580
  372.5 84.8 %copy-start.5 = (f32[1,2048]{1,0:T(1,128)S(1)}, f32[1,2048]{1,0:T(1,128)}, u32[]{:S(2)}) copy-start(f32[1,2048]{1,0:T(1,128)} %copy-done.4) | copy-start | bytes 24580
  372.6 84.8 %copy-start.7 = (f32[1,2048]{1,0:T(1,128)S(1)}, f32[1,2048]{1,0:T(1,128)}, u32[]{:S(2)}) copy-start(f32[1,2048]{1,0:T(1,128)} %copy-done.6) | copy-start | bytes 24580
  372.6 84.7 %copy-start.9 = (f32[1,2048]{1,0:T(1,128)S(1)}, f32[1,2048]{1,0:T(1,128)}, u32[]{:S(2)}) copy-start(f32[1,2048]{1,0:T(1,128)} %copy-done.8) | copy-start | bytes 24580
  372.6 84.7 %copy-start.11 = (f32[1,2048]{1,0:T(1,128)S(1)}, f32[1,2048]{1,0:T(1,128)}, u32[]{:S(2)}) copy-start(f32[1,2048]{1,0:T(1,128)} %copy-done.10) | copy-start | bytes 24580
  372.6 84.7 %copy-start.13 = (f32[1,2048]{1,0:T(1,128)S(1)}, f32[1,2048]{1,0:T(1,128)}, u32[]{:S(2)}) copy-start(f32[1,2048]{1,0:T(1,128)} %copy-done.12) | copy-start | bytes 24580
  372.6 84.7 %copy-start.15 = (f32[1,2048]{1,0:T(1,128)S(1)}, f32[1,2048]{1,0:T(1,128)}, u32[]{:S(2)}) copy-start(f32[1,2048]{1,0:T(1,128)} %copy-done.14) | copy-start | bytes 24580
  373.0 4.9 collective-permute-start.3
  373.7 4.3 collective-permute-start.2
Sparse Core Ops, SparseCore 0:
  10.4 68.3 all-gather.4
  81.1 63.0 all-gather.6
  346.6 99.6 reduce-scatter.6
  448.7 99.6 reduce-scatter.8
where the time goes:
time: 560 us; the launch traced here: 558 us
  waiting for transfers between devices  210 us (38%)
  matrix products  125 us (22%)
  local copies, waits for them, and re-layouts  116 us (21%)
  blocking collectives  78.2 us (14%)
  between operations  14.1 us (3%)
  other arithmetic  5.7 us (1%)
  starting transfers between devices  5.66 us (1%)
    unnamed x6, waiting for transfers between devices  86.6 us
    psum x1, blocking collectives, on_device(): filter_gradient = lax.psum(jnp.stack(filter_rows, 0), ('dp', 'seq'))  78.2 us
    all_gather x1, waiting for transfers between devices, on_device(): lax.all_gather(local_k, 'seq', axis=0, tiled=True)  65.4 us
    unnamed x46, local copies, waits for them, and re-layouts  62.6 us
    all_gather x1, waiting for transfers between devices, on_device(): lax.all_gather(local_v, 'seq', axis=0, tiled=True)  57.9 us
    dot_general x4, matrix products, forward_group(): jnp.einsum('htu,thd->uhd', dscore, q_part, preferred_element_type=jnp.flo...  38 us
    dot_general x4, matrix products, forward_group(): jnp.einsum('htu,uhd->thd', dscore, k_part, preferred_element_type=jnp.flo...  34.2 us
    dynamic_slice x20, local copies, waits for them, and re-layouts, columns(): lax.dynamic_slice_in_dim(matrix, group_index * group_width, group_width, 1)  27.5 us
  transfers between devices with their start and end apart: 8, of which 3 were waited for; matrix products, arithmetic and copies ran while one was open for 7% of the time, Pallas kernels for 0%

commit v1 on v0

--- a/solution.py
+++ b/solution.py
@@ -113,7 +113,7 @@
         moved = out_pad[tap_index : tap_index + tok_rows].astype(jnp.float32)
         conv_sum = conv_sum + filter_taps[tap_index] * moved
         filter_rows.append(jnp.sum(moved * local_gf, 0))
-    filter_gradient = lax.psum(jnp.stack(filter_rows, 0), ("dp", "seq"))
+    filter_gradient = jnp.sum(lax.all_gather(jnp.stack(filter_rows, 0), ("dp", "seq")), axis=0)
     conv_output = conv_sum.astype(jnp.bfloat16)
     return (
         conv_output[None],

time: 560 us -> 995 us (1.78)
  waiting for transfers between devices: 210 us -> 716 us
  blocking collectives: 78.2 us -> 0 us
    all_gather x0 -> x1, waiting for transfers between devices: none -> 430 us  [on_device(): lax.all_gather(jnp.stack(filter_rows, 0), ('dp', 'seq'))]
    psum x1 -> x0, blocking collectives: 78.2 us -> none  [on_device(): filter_gradient = lax.psum(jnp.stack(filter_rows, 0), ('dp', 'seq'))]
    unnamed x6 -> x7, waiting for transfers between devices: 86.6 us -> 163 us
    unnamed x46 -> x48, local copies, waits for them, and re-layouts: 62.6 us -> 62.5 us
  transfers between devices with their start and end apart: 8 -> 9, of which waited for: 3 -> 6; matrix products, arithmetic and copies ran while one was open for 7% -> 4% of each run, Pallas kernels for 0% -> 0%
where the time goes in v1:
time: 995 us; the launch traced here: 993 us
  waiting for transfers between devices  716 us (72%)
  matrix products  125 us (13%)
  local copies, waits for them, and re-layouts  116 us (12%)
  between operations  14.1 us (1%)
  other arithmetic  13.3 us (1%)
    all_gather x1, waiting for transfers between devices, on_device(): lax.all_gather(jnp.stack(filter_rows, 0), ('dp', 'seq'))  430 us
    unnamed x7, waiting for transfers between devices  163 us
    all_gather x1, waiting for transfers between devices, on_device(): lax.all_gather(local_k, 'seq', axis=0, tiled=True)  65.4 us
    unnamed x48, local copies, waits for them, and re-layouts  62.5 us
    all_gather x1, waiting for transfers between devices, on_device(): lax.all_gather(local_v, 'seq', axis=0, tiled=True)  57.9 us
    dot_general x4, matrix products, forward_group(): jnp.einsum('htu,thd->uhd', dscore, q_part, preferred_element_type=jnp.flo...  38 us
    dot_general x4, matrix products, forward_group(): jnp.einsum('htu,uhd->thd', dscore, k_part, preferred_element_type=jnp.flo...  34.2 us
    dynamic_slice x20, local copies, waits for them, and re-layouts, columns(): lax.dynamic_slice_in_dim(matrix, group_index * group_width, group_width, 1)  27.5 us
  transfers between devices with their start and end apart: 9, of which 6 were waited for; matrix products, arithmetic and copies ran while one was open for 4% of the time, Pallas kernels for 0%

profile of v1, /device:TPU:1, one launch (start us, length us, event | category | flops | bytes accessed | tf_op | source)
XLA Modules:
  0.0 993.2 jit_solution(4219799679103300817)
XLA Ops:
  7.2 2.1 copy.41
  9.4 2.0 copy.43
  12.3 2.8 collective-permute-start.1
  17.1 2.0 copy.42
  19.1 1.7 fusion.47
  20.9 57.9 %all-gather.8.cloned.1.call-done = bf16[1,2048,2048]{1,2,0:T(8,128)(2,1)} async-done(((bf16[1,128,2048]{1,2,0:T(8,128)(2,1)}), bf16[1,2048,2048]{1,2,0:T(8,128)(2,1)}) %all-gather.8.cloned.1.call-update) | async-done | bytes 8388624 | tf_op jit(solution)/shard_map/all_gather | solution.py:49
  78.7 65.4 %all-gather.10.cloned.1.call-done = bf16[1,2048,2048]{1,2,0:T(8,128)(2,1)} async-done(((bf16[1,128,2048]{1,2,0:T(8,128)(2,1)}), bf16[1,2048,2048]{1,2,0:T(8,128)(2,1)}) %all-gather.10.cloned.1.call-update) | async-done | bytes 8388624 | tf_op jit(solution)/shard_map/all_gather | solution.py:48
  144.2 177.3 %while.17 = (s32[]{:T(128)}, bf16[4,128,512]{1,2,0:T(8,128)(2,1)S(1)}, bf16[4,128,512]{1,2,0:T(8,128)(2,1)}, bf16[4,2048,512]{1,2,0:T(8,128)(2,1)}, bf16[4,2048,...) while((s32[]{:T(128)}, ...), condition=%wide.region_4.5_spmd.clone, body=%wide.region_0.4_spmd.clone.sunk | while | flops 1904614400 | bytes 82324224 | solution.py:95
  145.5 3.2 constant_dynamic-slice_fusion.8
  149.7 1.7 constant_dynamic-slice_fusion.10
  151.4 2.8 fusion.110
  155.4 6.5 fusion.111
  161.9 8.5 fusion.112
  170.5 3.1 convolution_convert_fusion.2
  175.1 9.5 fusion.114
  184.6 4.0 constant_dynamic-update-slice_fusion.7
  189.8 3.2 constant_dynamic-slice_fusion.8
  194.0 1.7 constant_dynamic-slice_fusion.10
  195.8 2.8 fusion.110
  199.7 6.5 fusion.111
  206.2 8.5 fusion.112
  214.8 3.1 convolution_convert_fusion.2
  219.4 9.5 fusion.114
  228.9 4.0 constant_dynamic-update-slice_fusion.7
  234.1 3.2 constant_dynamic-slice_fusion.8
  240.1 2.8 fusion.110
  244.1 6.5 fusion.111
  250.6 8.5 fusion.112
  259.1 3.1 convolution_convert_fusion.2
  263.7 9.5 fusion.114
  273.2 4.0 constant_dynamic-update-slice_fusion.7
  278.4 3.2 constant_dynamic-slice_fusion.8
  282.7 1.7 constant_dynamic-slice_fusion.10
  284.4 2.8 fusion.110
  288.3 6.5 fusion.111
  294.8 8.5 fusion.112
  303.4 3.1 convolution_convert_fusion.2
  308.0 9.5 fusion.114
  317.5 4.0 constant_dynamic-update-slice_fusion.7
  321.5 14.5 %copy.60 = bf16[4,2048,512]{2,0,1:T(4,128)(2,1)} copy(bf16[4,2048,512]{1,2,0:T(8,128)(2,1)} %get-tuple-element.67) | data formatting | bytes 16777216
  336.0 10.2 %copy.65 = bf16[256,8,4,512]{3,1,2,0:T(8,128)(2,1)} copy(bf16[256,8,4,512]{3,2,1,0:T(4,128)(2,1)} %bitcast.132) | data formatting | bytes 16777216
  346.3 14.6 %copy.62 = bf16[4,2048,512]{2,0,1:T(4,128)(2,1)} copy(bf16[4,2048,512]{1,2,0:T(8,128)(2,1)} %get-tuple-element.68) | data formatting | bytes 16777216
  360.9 10.2 %copy.66 = bf16[256,8,4,512]{3,1,2,0:T(8,128)(2,1)} copy(bf16[256,8,4,512]{3,2,1,0:T(4,128)(2,1)} %bitcast.133) | data formatting | bytes 16777216
  379.2 1.7 fusion.62
  381.0 64.5 %reduce-scatter.7.cloned.1.call-done = bf16[128,2048]{1,0:T(8,128)(2,1)} async-done(((bf16[2048,2048]{1,0:T(8,128)(2,1)}), bf16[128,2048]{1,0:T(8,128)(2,1)}) %reduce-scatter.7.cloned.1.call-update) | async-done | bytes 524304
  448.3 98.4 %reduce-scatter.9.cloned.1.call-done = bf16[128,2048]{1,0:T(8,128)(2,1)} async-done(((bf16[2048,2048]{1,0:T(8,128)(2,1)}), bf16[128,2048]{1,0:T(8,128)(2,1)}) %reduce-scatter.9.cloned.1.call-update) | async-done | bytes 524304
  549.5 429.5 %all-gather.12.cloned.1.call-done = f32[256,7,2048]{2,1,0:T(8,128)} async-done(((f32[1,7,2048]{2,1,0:T(8,128)}), f32[256,7,2048]{2,1,0:T(8,128)}) %all-gather.12.cloned.1.call-update) | async-done | bytes 14680080 | tf_op jit(solution)/shard_map/all_gather | solution.py:116
  979.1 7.6 reduce_sum.97
  (112 shorter events, 35.1 us)
Async XLA Ops:
  7.2 11.9 %copy-start = (bf16[1,128,2048]{2,1,0:T(8,128)(2,1)S(1)}, bf16[1,128,2048]{2,1,0:T(8,128)(2,1)}, u32[]{:S(2)}) copy-start(bf16[1,128,2048]{2,1,0:T(8,128)(2,1)} %param.10) | copy-start | bytes 1572868
  7.2 71.6 %all-gather.8.cloned.1.call-start = ((), (), s32[]{:S(2)}) async-start(), calls=%async_computation.2 | async-start | bytes 8912896 | tf_op jit(solution)/shard_map/all_gather | solution.py:49
  9.3 134.8 %all-gather.10.cloned.1.call-start = ((), (), s32[]{:S(2)}) async-start(), calls=%async_computation.3 | async-start | bytes 8912896 | tf_op jit(solution)/shard_map/all_gather | solution.py:48
  11.5 434.0 %reduce-scatter.7.cloned.1.call-start = ((), (), s32[]{:S(2)}) async-start(), calls=%async_computation.5 | async-start | bytes 8912896
  12.3 6.8 collective-permute-start.1
  15.1 4.0 collective-permute-start
  16.9 127.2 %copy-start.3 = (f32[1,2048]{1,0:T(1,128)}, f32[1,2048]{1,0:T(1,128)S(1)}, u32[]{:S(2)}) copy-start(f32[1,2048]{1,0:T(1,128)S(1)} %get-tuple-element.162) | copy-start | bytes 24580
  16.9 127.2 %copy-start.5 = (f32[1,2048]{1,0:T(1,128)}, f32[1,2048]{1,0:T(1,128)S(1)}, u32[]{:S(2)}) copy-start(f32[1,2048]{1,0:T(1,128)S(1)} %get-tuple-element.163) | copy-start | bytes 24580
  16.9 127.2 %copy-start.7 = (f32[1,2048]{1,0:T(1,128)}, f32[1,2048]{1,0:T(1,128)S(1)}, u32[]{:S(2)}) copy-start(f32[1,2048]{1,0:T(1,128)S(1)} %get-tuple-element.164) | copy-start | bytes 24580
  17.0 127.2 %copy-start.9 = (f32[1,2048]{1,0:T(1,128)}, f32[1,2048]{1,0:T(1,128)S(1)}, u32[]{:S(2)}) copy-start(f32[1,2048]{1,0:T(1,128)S(1)} %get-tuple-element.165) | copy-start | bytes 24580
  17.0 127.2 %copy-start.11 = (f32[1,2048]{1,0:T(1,128)}, f32[1,2048]{1,0:T(1,128)S(1)}, u32[]{:S(2)}) copy-start(f32[1,2048]{1,0:T(1,128)S(1)} %get-tuple-element.166) | copy-start | bytes 24580
  17.0 127.2 %copy-start.13 = (f32[1,2048]{1,0:T(1,128)}, f32[1,2048]{1,0:T(1,128)S(1)}, u32[]{:S(2)}) copy-start(f32[1,2048]{1,0:T(1,128)S(1)} %get-tuple-element.167) | copy-start | bytes 24580
  17.0 127.2 %copy-start.15 = (f32[1,2048]{1,0:T(1,128)}, f32[1,2048]{1,0:T(1,128)S(1)}, u32[]{:S(2)}) copy-start(f32[1,2048]{1,0:T(1,128)S(1)} %get-tuple-element.168) | copy-start | bytes 24580
  170.4 3.8 copy-start.17
  214.8 3.8 copy-start.17
  259.1 3.8 copy-start.17
  303.4 3.8 copy-start.17
  346.3 200.4 %reduce-scatter.9.cloned.1.call-start = ((), (), s32[]{:S(2)}) async-start(), calls=%async_computation.6 | async-start | bytes 8912896
  371.2 1.0 copy-start.1
  371.2 607.9 %all-gather.12.cloned.1.call-start = ((), (), s32[]{:S(2)}) async-start(), calls=%async_computation.4 | async-start | bytes 16842752 | tf_op jit(solution)/shard_map/all_gather | solution.py:116
  372.4 6.8 copy-start.4
  372.4 6.8 copy-start.6
  372.4 6.8 copy-start.8
  372.4 6.8 copy-start.10
  372.5 6.7 copy-start.12
  372.5 6.7 copy-start.14
  372.5 6.7 copy-start.16
  372.9 5.2 copy-start.2
  372.9 3.5 collective-permute-start.3
  373.6 2.8 collective-permute-start.2
Sparse Core Ops, SparseCore 0:
  10.4 68.3 all-gather.7
  81.1 63.0 all-gather.9
  346.4 98.9 reduce-scatter.6
  447.8 98.8 reduce-scatter.8
  549.0 430.0 all-gather.11
